TPU v7x, 32 devices: a whole 2x2x4 slice. The times are simulated.
32 devices in a mesh: blk: 8 (over y, x, core), head: 4 (over z).
Axes of the slice: x: 2, y: 2, z: 4, core: 2. Of those that a mesh axis runs over, the one named last changes fastest.
Arguments:
- query_matrix: bfloat16 [4096, 4096], P(('blk', 'head')), may hold values from -6 to 6
- key_matrix: bfloat16 [4096, 512], P(('blk', 'head')), may hold values from -6 to 6
- value_matrix: bfloat16 [4096, 512], P(('blk', 'head')), may hold values from -6 to 6
- output_cotangent: bfloat16 [4096, 4096], P(('blk', 'head')), may hold values from -6 to 6
- forward_output: bfloat16 [4096, 4096], P(('blk', 'head')), may hold values from -6 to 6
- doc_ids: int32 [4096], P(('blk', 'head')), may hold values from 0 to 31, never falling along the last dimension, each value on 1 to 2048 neighbouring positions
Outputs:
- query_grad: bfloat16 [4096, 4096], P(('blk', 'head'))
- key_gradient: bfloat16 [4096, 512], P(('blk', 'head'))
- value_gradient: bfloat16 [4096, 512], P(('blk', 'head'))
Inputs may be any that keep to these rules, and one draw needn't show every extreme that they name: `doc_ids`: document numbers never fall along the window; every document has 2048 tokens or fewer and one has exactly 2048.
All inputs are finite; a program needn't handle non-finite values.
Results may differ from a plain program's by a relative error of at most 0.0051.
Values may be sent and summed in bfloat16 or wider, within the bound.
No kernel may reach another device: no remote copies, remote signals or barrier semaphores. Data moves between devices by JAX's collectives and lax.ppermute only.
A program may use at most 64 MiB of HBM per device.

v0:
```python
import jax
import jax.numpy as jnp
from jax import lax
from jax.sharding import PartitionSpec as P

HEAD_WIDTH = 128
DOC_SPAN = 4
masked_score = -1e30


def shifted(block, axis, distance):
    devices = range(lax.axis_size(axis))
    route = [(i - distance, i) for i in devices if i - distance in devices]
    return lax.ppermute(block, axis, route)


def passed_along(block, axis, distance):
    devices = range(lax.axis_size(axis))
    route = [((i - distance) % len(devices), i) for i in devices]
    return lax.ppermute(block, axis, route)


def per_device(query_matrix, key_matrix, value_matrix, output_cotangent, forward_output, doc_ids):
    cycle_size = lax.axis_size("blk")
    head_ways = lax.axis_size("head")
    block_rows = query_matrix.shape[0] * head_ways
    query_heads = query_matrix.shape[1] // (HEAD_WIDTH * head_ways)
    kv_heads = key_matrix.shape[1] // (HEAD_WIDTH * head_ways)
    heads_per_group = query_heads // kv_heads
    logit_scale = HEAD_WIDTH ** (-0.5)
    query_local, grad_local, output_local, key_local, value_local = (
        lax.all_to_all(query_matrix, "head", split_axis=1, concat_axis=0, tiled=True),
        lax.all_to_all(output_cotangent, "head", split_axis=1, concat_axis=0, tiled=True),
        lax.all_to_all(forward_output, "head", split_axis=1, concat_axis=0, tiled=True),
        lax.all_to_all(key_matrix, "head", split_axis=1, concat_axis=0, tiled=True),
        lax.all_to_all(value_matrix, "head", split_axis=1, concat_axis=0, tiled=True),
    )
    all_segments = lax.all_gather(doc_ids, ("blk", "head"), axis=0, tiled=True)
    my_block = lax.axis_index("blk")
    query_tensor = query_local.reshape(block_rows, kv_heads, heads_per_group, HEAD_WIDTH)
    returned_grads = grad_local.reshape(block_rows, kv_heads, heads_per_group, HEAD_WIDTH)
    stored_output = output_local.reshape(block_rows, kv_heads, heads_per_group, HEAD_WIDTH)
    row_terms = jnp.sum(
        returned_grads.astype(jnp.float32) * stored_output.astype(jnp.float32), axis=-1
    ).transpose(1, 2, 0)[..., None]
    query_segment = lax.dynamic_slice_in_dim(all_segments, my_block * block_rows, block_rows, 0)
    query_position = my_block * block_rows + jnp.arange(block_rows, dtype=jnp.int32)
    first_segment = all_segments[my_block * block_rows]

    def shares_doc(anchor):
        last_segment = all_segments[jnp.maximum(anchor, 0) * block_rows + block_rows - 1]
        return (anchor == my_block) | (anchor >= 0) & (anchor < my_block) & (
            last_segment == first_segment
        )

    def block_scores(key_block, anchor):
        key_split = key_block.reshape(block_rows, kv_heads, HEAD_WIDTH)
        key_segment = lax.dynamic_slice_in_dim(
            all_segments, jnp.maximum(anchor, 0) * block_rows, block_rows, 0
        )
        key_position = anchor * block_rows + jnp.arange(block_rows, dtype=jnp.int32)
        allowed = (query_segment[:, None] == key_segment[None, :]) & (
            key_position[None, :] <= query_position[:, None]
        )
        scores = (
            jnp.einsum(
                "ighd,jgd->ghij", query_tensor, key_split, preferred_element_type=jnp.float32
            )
            * logit_scale
        )
        return (jnp.where(allowed, scores, masked_score), allowed)

    def add_stats(running, key_block, anchor):
        run_max, run_sum = running
        scores, allowed = block_scores(key_block, anchor)
        new_max = jnp.maximum(run_max, jnp.max(scores, axis=-1, keepdims=True))
        new_sum = run_sum * jnp.exp(run_max - new_max) + jnp.sum(
            jnp.where(allowed, jnp.exp(scores - new_max), 0.0), axis=-1, keepdims=True
        )
        return (new_max, new_sum)

    near_blocks = [(key_local, value_local, my_block, 0)]
    for distance in range(1, min(DOC_SPAN, cycle_size - 1) + 1):
        near_key, near_value = shifted((key_local, value_local), "blk", distance)
        near_blocks.append((near_key, near_value, my_block - distance, distance))
    start_max = jnp.full((kv_heads, heads_per_group, block_rows, 1), masked_score, jnp.float32)
    start_sum = jnp.zeros((kv_heads, heads_per_group, block_rows, 1), jnp.float32)
    running = (start_max, start_sum)
    for near_key, near_value, anchor, distance in near_blocks:
        running = lax.cond(
            shares_doc(anchor),
            lambda inner, kb=near_key, og=anchor: add_stats(inner, kb, og),
            lambda inner: inner,
            running,
        )
    run_max, run_sum = running
    log_total = run_max + jnp.log(run_sum)

    def block_grads(operands):
        key_block, value_block, anchor = operands
        scores, allowed = block_scores(key_block, anchor)
        key_split = key_block.reshape(block_rows, kv_heads, HEAD_WIDTH)
        value_split = value_block.reshape(block_rows, kv_heads, HEAD_WIDTH)
        probabilities = jnp.where(allowed, jnp.exp(scores - log_total), 0.0)
        prob_grad = jnp.einsum(
            "ighd,jgd->ghij", returned_grads, value_split, preferred_element_type=jnp.float32
        )
        score_grad = (probabilities * (prob_grad - row_terms)).astype(jnp.bfloat16)
        weights_half = probabilities.astype(jnp.bfloat16)
        value_part = jnp.einsum(
            "ghij,ighd->jgd", weights_half, returned_grads, preferred_element_type=jnp.float32
        )
        key_part = jnp.einsum(
            "ghij,ighd->jgd", score_grad, query_tensor, preferred_element_type=jnp.float32
        )
        query_part = jnp.einsum(
            "ghij,jgd->ighd", score_grad, key_split, preferred_element_type=jnp.float32
        )
        return (
            query_part.reshape(block_rows, query_heads * HEAD_WIDTH),
            key_part.reshape(block_rows, kv_heads * HEAD_WIDTH),
            value_part.reshape(block_rows, kv_heads * HEAD_WIDTH),
        )

    def empty_grads(operands):
        return (
            jnp.zeros((block_rows, query_heads * HEAD_WIDTH), jnp.float32),
            jnp.zeros((block_rows, kv_heads * HEAD_WIDTH), jnp.float32),
            jnp.zeros((block_rows, kv_heads * HEAD_WIDTH), jnp.float32),
        )

    def maybe_grads(key_block, value_block, anchor):
        return lax.cond(
            shares_doc(anchor), block_grads, empty_grads, (key_block, value_block, anchor)
        )

    def pass_grads(grad_pair):
        return passed_along((grad_pair[0], grad_pair[1]), "blk", -1)

    def turn_step(turn_index, carried):
        key_block, value_block, query_total, summed_key_grad, summed_value_grad = carried
        anchor = (my_block + turn_index) % cycle_size
        query_part, key_part, value_part = maybe_grads(key_block, value_block, anchor)
        summed_key_grad, summed_value_grad = pass_grads(
            (summed_key_grad + key_part, summed_value_grad + value_part)
        )
        key_block, value_block = passed_along((key_block, value_block), "blk", -1)
        return (
            key_block,
            value_block,
            query_total + query_part,
            summed_key_grad,
            summed_value_grad,
        )

    starting_state = (
        key_local,
        value_local,
        jnp.zeros((block_rows, query_heads * HEAD_WIDTH), jnp.float32),
        jnp.zeros((block_rows, kv_heads * HEAD_WIDTH), jnp.float32),
        jnp.zeros((block_rows, kv_heads * HEAD_WIDTH), jnp.float32),
    )
    key_block, value_block, query_total, summed_key_grad, summed_value_grad = lax.fori_loop(
        0, cycle_size - 1, turn_step, starting_state
    )
    anchor = (my_block + (cycle_size - 1)) % cycle_size
    query_part, key_part, value_part = maybe_grads(key_block, value_block, anchor)
    query_total = query_total + query_part
    summed_key_grad, summed_value_grad = pass_grads(
        (summed_key_grad + key_part, summed_value_grad + value_part)
    )
    query_grad = (query_total * logit_scale).astype(jnp.bfloat16)
    key_gradient = (summed_key_grad * logit_scale).astype(jnp.bfloat16)
    value_gradient = summed_value_grad.astype(jnp.bfloat16)
    return (
        lax.all_to_all(query_grad, "head", split_axis=0, concat_axis=1, tiled=True),
        lax.all_to_all(key_gradient, "head", split_axis=0, concat_axis=1, tiled=True),
        lax.all_to_all(value_gradient, "head", split_axis=0, concat_axis=1, tiled=True),
    )


def solution(mesh):
    return jax.shard_map(
        per_device,
        mesh=mesh,
        in_specs=(
            P(("blk", "head"), None),
            P(("blk", "head"), None),
            P(("blk", "head"), None),
            P(("blk", "head"), None),
            P(("blk", "head"), None),
            P(("blk", "head")),
        ),
        out_specs=(P(("blk", "head"), None), P(("blk", "head"), None), P(("blk", "head"), None)),
        check_vma=False,
    )
```

profile of v0, /device:TPU:6, one launch (start us, length us, event | category | flops | bytes accessed | tf_op | source)
XLA Modules:
  0.0 454.4 jit_solution(7301382656809553807)
XLA Ops:
  2.2 4.9 %all-to-all-start = ((bf16[128,4,128]{2,0,1:T(8,128)(2,1)}), bf16[128,4,128]{2,0,1:T(8,128)(2,1)}, u32[]{:S(2)}, u32[]{:S(2)}) async-start(bf16[128,4,128]{2,0,1:T(8,128)(2,1)} %copy_bitcast_fusion.4), calls=%async_computation | async-start | bytes 262144 | tf_op jit(solution)/shard_map/all_to_all | solution.py:35
  7.1 2.3 copy.157
  9.4 3.9 all-to-all-done
  13.3 3.5 all-to-all-start.2
  16.8 2.3 copy.156
  19.1 22.1 %all-to-all-done.2 = bf16[128,4,1024]{2,0,1:T(8,128)(2,1)S(1)} async-done(((bf16[128,4,1024]{2,0,1:T(8,128)(2,1)}), bf16[128,4,1024]{2,0,1:T(8,128)(2,1)S(1)}, u32[]{:S(2)}, u32[]{:S(2)}) %all-to-all-start.2) | async-done | bytes 1048608 | tf_op jit(solution)/shard_map/all_to_all | solution.py:32
  41.2 3.5 all-to-all-start.3
  45.8 24.1 %all-to-all-done.3 = bf16[128,4,1024]{2,0,1:T(8,128)(2,1)S(1)} async-done(((bf16[128,4,1024]{2,0,1:T(8,128)(2,1)}), bf16[128,4,1024]{2,0,1:T(8,128)(2,1)S(1)}, u32[]{:S(2)}, u32[]{:S(2)}) %all-to-all-start.3) | async-done | bytes 1048608 | tf_op jit(solution)/shard_map/all_to_all | solution.py:33
  69.9 4.2 all-to-all-start.4
  74.3 75.4 %all-gather = s32[32,1,128]{2,1,0:T(1,128)S(1)} all-gather(s32[1,1,128]{2,1,0:T(1,128)S(1)} %bitcast.369), channel_id=1, replica_groups=mesh['blk'=8,'head'=4] {'blk','head'}, dimensions={0}, use_global_device_ids=true | all-gather | bytes 16896 | tf_op jit(solution)/shard_map/all_gather | solution.py:38
  168.2 5.6 %all-to-all-start.1 = ((bf16[128,4,128]{2,0,1:T(8,128)(2,1)}), bf16[128,4,128]{2,0,1:T(8,128)(2,1)}, u32[]{:S(2)}, u32[]{:S(2)}) async-start(bf16[128,4,128]{2,0,1:T(8,128)(2,1)} %copy_bitcast_fusion.3), calls=%async_computation.1 | async-start | bytes 262144 | tf_op jit(solution)/shard_map/all_to_all | solution.py:36
  178.8 2.5 fusion.78
  181.3 2.0 select_reduce_fusion.4
  183.4 5.7 %conditional.6 = ((f32[1,8,512,1]{2,1,3,0:T(8,128)S(1)}, f32[1,8,512,1]{2,1,3,0:T(8,128)S(1)})) conditional(s32[]{:T(128)} %convert_element_type.80, (f32[1,8,512,1]{2,1,3,0:T(8,128)S(1)}, f32[1,8,512,1]{2,1,3,0:T(8,128)S(1)}) %tuple.89, (s32[512]{0:T(512)S(1)}, s32[]{:T(128)}, s32[4096]{0:T(1024)}, s32[512]{0:T(512)S(1)}, ...), branch_computations={%region_2.3_spmd, %region_3.6_spmd} | conditional | flops 554443264 | bytes 18970726 | solution.py:90
  184.4 2.5 fusion.2
  187.0 2.0 select_reduce_fusion
  191.6 188.0 %while.26 = (s32[]{:T(128)}, bf16[512,128]{0,1:T(8,128)(2,1)S(1)}, bf16[512,128]{1,0:T(8,128)(2,1)}, f32[512,1024]{0,1:T(8,128)}, f32[512,128]{1,0:T(8,128)}, /*...) while((s32[]{:T(128)}, bf16[512,128]{0,1:T(8,128)(2,1)S(1)}, ...), condition=%wide.region_22.23_spmd.clone, body=%wide.region_19.22_spmd.clone.sunk | while | flops 2711487488 | bytes 62722972 | solution.py:163
  192.2 18.7 %collective-permute-start = (bf16[512,128]{0,1:T(8,128)(2,1)}, bf16[512,128]{0,1:T(8,128)(2,1)S(1)}, u32[]{:S(2)}, u32[]{:S(2)}) collective-permute-start(bf16[512,128]{0,1:T(8,128)(2,1)} %copy.187), channel_id=1, source_target_pairs={{4,0},{8,4},{12,8},{16,12},{20,16},{24,20},{28,24},{0,28},{5,1},{9... | collective-permute-start | bytes 393224 | tf_op jit(solution)/shard_map/while/body/eval_jaxpr/ppermute | solution.py:20
  214.9 13.2 %conditional.13 = (f32[512,1024]{0,1:T(8,128)S(1)}, f32[512,128]{1,0:T(8,128)}, f32[512,128]{1,0:T(8,128)S(1)}) conditional(s32[]{:T(128)} %convert_element_type.114, () %tuple.152, (s32[512]{0:T(512)S(1)}, s32[]{:T(128)}, s32[4096]{0:T(1024)}, s32[]{:T(128)}, bf16[512,1,8,128]{3,0,2,1:T(8,128)(2,1)S(1)}, /*index=5*/bf16[512,128]{0,1:T(8,128)(2,1)}, ...), branch_computations={%region_20.20_spmd, %region_21.21_spmd} | conditional | flops 2710307840 | bytes 50137280 | solution.py:133
  216.1 2.2 fusion.39
  218.3 2.1 fusion.33
  220.4 4.2 fusion.29
  234.1 2.8 collective-permute-done.2
  248.1 3.4 select_add_fusion.2
  263.0 2.8 collective-permute-start.3
  268.6 3.4 select_add_fusion.2
  283.2 2.8 collective-permute-start.3
  287.8 3.4 select_add_fusion.2
  302.3 13.1 %collective-permute-start.3 = (f32[512,128]{1,0:T(8,128)}, f32[512,128]{1,0:T(8,128)S(1)}, u32[]{:S(2)}, u32[]{:S(2)}) collective-permute-start(f32[512,128]{1,0:T(8,128)} %add.386), channel_id=1, source_target_pairs={{4,0},{8,4},{12,8},{16,12},{20,16},{24,20},{28,24},{0,28},{5,1},{9... | collective-permute-start | bytes 786440 | tf_op jit(solution)/shard_map/while/body/eval_jaxpr/ppermute | solution.py:20
  317.2 3.4 select_add_fusion.2
  331.8 12.2 %collective-permute-start.3 = (f32[512,128]{1,0:T(8,128)}, f32[512,128]{1,0:T(8,128)S(1)}, u32[]{:S(2)}, u32[]{:S(2)}) collective-permute-start(f32[512,128]{1,0:T(8,128)} %add.386), channel_id=1, source_target_pairs={{4,0},{8,4},{12,8},{16,12},{20,16},{24,20},{28,24},{0,28},{5,1},{9... | collective-permute-start | bytes 786440 | tf_op jit(solution)/shard_map/while/body/eval_jaxpr/ppermute | solution.py:20
  345.8 3.4 select_add_fusion.2
  360.3 12.3 %collective-permute-start.3 = (f32[512,128]{1,0:T(8,128)}, f32[512,128]{1,0:T(8,128)S(1)}, u32[]{:S(2)}, u32[]{:S(2)}) collective-permute-start(f32[512,128]{1,0:T(8,128)} %add.386), channel_id=1, source_target_pairs={{4,0},{8,4},{12,8},{16,12},{20,16},{24,20},{28,24},{0,28},{5,1},{9... | collective-permute-start | bytes 786440 | tf_op jit(solution)/shard_map/while/body/eval_jaxpr/ppermute | solution.py:20
  374.4 3.4 select_add_fusion.2
  379.6 16.7 %conditional.10 = (f32[512,1024]{0,1:T(8,128)}, f32[512,128]{1,0:T(8,128)}, f32[512,128]{1,0:T(8,128)}) conditional(s32[]{:T(128)} %convert_element_type.85, () %tuple.95, (s32[512]{0:T(512)S(1)}, s32[]{:T(128)}, s32[4096]{0:T(1024)}, s32[512]{0:T(512)S(1)}, bf16[512,1,8,128]{3,2,0,1:T(8,128)(2,1)}, /*index=5*/bf16[512,128]{0,1:T(8,128)(2,1)S(1)}, ...), branch_computations={%region_23.24_spmd, %region_24.25_spmd} | conditional | flops 2710307328 | bytes 54360276 | solution.py:133
  382.5 2.5 fusion.65
  385.0 2.9 fusion.59
  387.9 4.4 fusion.55
  394.3 2.1 fusion.72
  397.4 2.2 collective-permute-start.8
  400.7 4.2 collective-permute-done.9
  405.0 4.8 %all-to-all-start.7 = ((bf16[4,128,128]{2,1,0:T(8,128)(2,1)}), bf16[4,128,128]{2,1,0:T(8,128)(2,1)S(1)}, u32[]{:S(2)}, u32[]{:S(2)}) async-start(bf16[4,128,128]{2,1,0:T(8,128)(2,1)} %bitcast.98), calls=%async_computation.7 | async-start | bytes 262144 | tf_op jit(solution)/shard_map/all_to_all | solution.py:178
  410.5 5.5 %all-to-all-done.7 = bf16[4,128,128]{2,1,0:T(8,128)(2,1)S(1)} async-done(((bf16[4,128,128]{2,1,0:T(8,128)(2,1)}), bf16[4,128,128]{2,1,0:T(8,128)(2,1)S(1)}, u32[]{:S(2)}, u32[]{:S(2)}) %all-to-all-start.7) | async-done | bytes 131104 | tf_op jit(solution)/shard_map/all_to_all | solution.py:178
  416.0 3.3 all-to-all-start.6
  419.3 2.1 multiply_convert_fusion
  422.8 2.4 all-to-all-done.6
  425.2 3.5 all-to-all-start.5
  430.5 21.9 %all-to-all-done.5 = bf16[4,128,1024]{2,1,0:T(8,128)(2,1)S(1)} async-done(((bf16[4,128,1024]{2,1,0:T(8,128)(2,1)}), bf16[4,128,1024]{2,1,0:T(8,128)(2,1)S(1)}, u32[]{:S(2)}, u32[]{:S(2)}) %all-to-all-start.5) | async-done | bytes 1048608 | tf_op jit(solution)/shard_map/all_to_all | solution.py:176
  (229 shorter events, 127.3 us)
Async XLA Ops:
  0.6 44.1 %copy-start.10 = (bf16[128,4096]{1,0:T(8,128)(2,1)S(1)}, bf16[128,4096]{1,0:T(8,128)(2,1)}, u32[]{:S(2)}) copy-start(bf16[128,4096]{1,0:T(8,128)(2,1)} %param.24) | copy-start | bytes 3145732
  0.7 73.6 %copy-start.18 = (s32[128]{0:T(128)S(1)}, s32[128]{0:T(128)}, u32[]{:S(2)}) copy-start(s32[128]{0:T(128)} %param.25) | copy-start | bytes 1540
  1.5 155.4 %copy-start.12 = (bf16[128,512]{1,0:T(8,128)(2,1)S(1)}, bf16[128,512]{1,0:T(8,128)(2,1)}, u32[]{:S(2)}) copy-start(bf16[128,512]{1,0:T(8,128)(2,1)} %param.22) | copy-start | bytes 393220
  2.2 11.1 %all-to-all-start = ((bf16[128,4,128]{2,0,1:T(8,128)(2,1)}), bf16[128,4,128]{2,0,1:T(8,128)(2,1)}, u32[]{:S(2)}, u32[]{:S(2)}) async-start(bf16[128,4,128]{2,0,1:T(8,128)(2,1)} %copy_bitcast_fusion.4), calls=%async_computation | async-start | bytes 262144 | tf_op jit(solution)/shard_map/all_to_all | solution.py:35
  13.3 28.0 %all-to-all-start.2 = ((bf16[128,4,1024]{2,0,1:T(8,128)(2,1)}), bf16[128,4,1024]{2,0,1:T(8,128)(2,1)S(1)}, u32[]{:S(2)}, u32[]{:S(2)}) async-start(bf16[128,4,1024]{2,0,1:T(8,128)(2,1)} %bitcast.326), calls=%async_computation.2 | async-start | bytes 2097152 | tf_op jit(solution)/shard_map/all_to_all | solution.py:32
  41.2 28.7 %all-to-all-start.3 = ((bf16[128,4,1024]{2,0,1:T(8,128)(2,1)}), bf16[128,4,1024]{2,0,1:T(8,128)(2,1)S(1)}, u32[]{:S(2)}, u32[]{:S(2)}) async-start(bf16[128,4,1024]{2,0,1:T(8,128)(2,1)} %bitcast.325), calls=%async_computation.3 | async-start | bytes 2097152 | tf_op jit(solution)/shard_map/all_to_all | solution.py:33
  69.9 95.3 %copy-start.9 = (bf16[128,4,1024]{2,0,1:T(8,128)(2,1)}, bf16[128,4,1024]{2,0,1:T(8,128)(2,1)S(1)}, u32[]{:S(2)}) copy-start(bf16[128,4,1024]{2,0,1:T(8,128)(2,1)S(1)} %all-to-all-done.3) | copy-start | bytes 3145732
  69.9 98.3 %all-to-all-start.4 = ((bf16[128,4,1024]{2,0,1:T(8,128)(2,1)}), bf16[128,4,1024]{2,0,1:T(8,128)(2,1)}, u32[]{:S(2)}, u32[]{:S(2)}) async-start(bf16[128,4,1024]{2,0,1:T(8,128)(2,1)} %bitcast.324), calls=%async_computation.4 | async-start | bytes 2097152 | tf_op jit(solution)/shard_map/all_to_all | solution.py:34
  158.9 30.3 %collective-permute-start.7 = (bf16[512,128]{1,0:T(8,128)(2,1)}, bf16[512,128]{1,0:T(8,128)(2,1)}, u32[]{:S(2)}, u32[]{:S(2)}) collective-permute-start(bf16[512,128]{1,0:T(8,128)(2,1)} %bitcast.67), channel_id=1, source_target_pairs={{0,16},{4,20},{8,24},{12,28},{1,17},{5,21},{9,25},{13,29},{2,18},{... | collective-permute-start | bytes 393224 | tf_op jit(solution)/shard_map/ppermute | solution.py:14
  160.2 29.0 %collective-permute-start.6 = (bf16[512,128]{1,0:T(8,128)(2,1)}, bf16[512,128]{1,0:T(8,128)(2,1)}, u32[]{:S(2)}, u32[]{:S(2)}) collective-permute-start(bf16[512,128]{1,0:T(8,128)(2,1)} %bitcast.67), channel_id=1, source_target_pairs={{0,12},{4,16},{8,20},{12,24},{16,28},{1,13},{5,17},{9,21},{13,25},... | collective-permute-start | bytes 393224 | tf_op jit(solution)/shard_map/ppermute | solution.py:14
  161.5 27.5 %collective-permute-start.5 = (bf16[512,128]{1,0:T(8,128)(2,1)}, bf16[512,128]{1,0:T(8,128)(2,1)}, u32[]{:S(2)}, u32[]{:S(2)}) collective-permute-start(bf16[512,128]{1,0:T(8,128)(2,1)} %bitcast.67), channel_id=1, source_target_pairs={{0,8},{4,12},{8,16},{12,20},{16,24},{20,28},{1,9},{5,13},{9,17},{1... | collective-permute-start | bytes 393224 | tf_op jit(solution)/shard_map/ppermute | solution.py:14
  162.8 20.5 %collective-permute-start.4 = (bf16[512,128]{1,0:T(8,128)(2,1)}, bf16[512,128]{1,0:T(8,128)(2,1)}, u32[]{:S(2)}, u32[]{:S(2)}) collective-permute-start(bf16[512,128]{1,0:T(8,128)(2,1)} %bitcast.67), channel_id=1, source_target_pairs={{0,4},{4,8},{8,12},{12,16},{16,20},{20,24},{24,28},{1,5},{5,9},{9,... | collective-permute-start | bytes 393224 | tf_op jit(solution)/shard_map/ppermute | solution.py:14
  168.2 21.9 %all-to-all-start.1 = ((bf16[128,4,128]{2,0,1:T(8,128)(2,1)}), bf16[128,4,128]{2,0,1:T(8,128)(2,1)}, u32[]{:S(2)}, u32[]{:S(2)}) async-start(bf16[128,4,128]{2,0,1:T(8,128)(2,1)} %copy_bitcast_fusion.3), calls=%async_computation.1 | async-start | bytes 262144 | tf_op jit(solution)/shard_map/all_to_all | solution.py:36
  192.2 41.2 %collective-permute-start = (bf16[512,128]{0,1:T(8,128)(2,1)}, bf16[512,128]{0,1:T(8,128)(2,1)S(1)}, u32[]{:S(2)}, u32[]{:S(2)}) collective-permute-start(bf16[512,128]{0,1:T(8,128)(2,1)} %copy.187), channel_id=1, source_target_pairs={{4,0},{8,4},{12,8},{16,12},{20,16},{24,20},{28,24},{0,28},{5,1},{9... | collective-permute-start | bytes 393224 | tf_op jit(solution)/shard_map/while/body/eval_jaxpr/ppermute | solution.py:20
  212.5 21.0 %collective-permute-start.1 = (bf16[512,128]{1,0:T(8,128)(2,1)}, bf16[512,128]{1,0:T(8,128)(2,1)}, u32[]{:S(2)}, u32[]{:S(2)}) collective-permute-start(bf16[512,128]{1,0:T(8,128)(2,1)} %copy.188), channel_id=1, source_target_pairs={{4,0},{8,4},{12,8},{16,12},{20,16},{24,20},{28,24},{0,28},{5,1},{9... | collective-permute-start | bytes 393224 | tf_op jit(solution)/shard_map/while/body/eval_jaxpr/ppermute | solution.py:20
  229.9 4.2 collective-permute-start.3
  231.6 5.3 %collective-permute-start.2 = (f32[512,128]{1,0:T(8,128)}, f32[512,128]{1,0:T(8,128)}, u32[]{:S(2)}, u32[]{:S(2)}) collective-permute-start(f32[512,128]{1,0:T(8,128)} %add.385), channel_id=1, source_target_pairs={{4,0},{8,4},{12,8},{16,12},{20,16},{24,20},{28,24},{0,28},{5,1},{9... | collective-permute-start | bytes 786440 | tf_op jit(solution)/shard_map/while/body/eval_jaxpr/ppermute | solution.py:20
  237.5 14.0 %collective-permute-start = (bf16[512,128]{0,1:T(8,128)(2,1)}, bf16[512,128]{0,1:T(8,128)(2,1)S(1)}, u32[]{:S(2)}, u32[]{:S(2)}) collective-permute-start(bf16[512,128]{0,1:T(8,128)(2,1)} %copy.187), channel_id=1, source_target_pairs={{4,0},{8,4},{12,8},{16,12},{20,16},{24,20},{28,24},{0,28},{5,1},{9... | collective-permute-start | bytes 393224 | tf_op jit(solution)/shard_map/while/body/eval_jaxpr/ppermute | solution.py:20
  241.0 10.5 %collective-permute-start.1 = (bf16[512,128]{1,0:T(8,128)(2,1)}, bf16[512,128]{1,0:T(8,128)(2,1)}, u32[]{:S(2)}, u32[]{:S(2)}) collective-permute-start(bf16[512,128]{1,0:T(8,128)(2,1)} %copy.188), channel_id=1, source_target_pairs={{4,0},{8,4},{12,8},{16,12},{20,16},{24,20},{28,24},{0,28},{5,1},{9... | collective-permute-start | bytes 393224 | tf_op jit(solution)/shard_map/while/body/eval_jaxpr/ppermute | solution.py:20
  246.2 5.3 %collective-permute-start.3 = (f32[512,128]{1,0:T(8,128)}, f32[512,128]{1,0:T(8,128)S(1)}, u32[]{:S(2)}, u32[]{:S(2)}) collective-permute-start(f32[512,128]{1,0:T(8,128)} %add.386), channel_id=1, source_target_pairs={{4,0},{8,4},{12,8},{16,12},{20,16},{24,20},{28,24},{0,28},{5,1},{9... | collective-permute-start | bytes 786440 | tf_op jit(solution)/shard_map/while/body/eval_jaxpr/ppermute | solution.py:20
  248.1 5.3 %collective-permute-start.2 = (f32[512,128]{1,0:T(8,128)}, f32[512,128]{1,0:T(8,128)}, u32[]{:S(2)}, u32[]{:S(2)}) collective-permute-start(f32[512,128]{1,0:T(8,128)} %add.385), channel_id=1, source_target_pairs={{4,0},{8,4},{12,8},{16,12},{20,16},{24,20},{28,24},{0,28},{5,1},{9... | collective-permute-start | bytes 786440 | tf_op jit(solution)/shard_map/while/body/eval_jaxpr/ppermute | solution.py:20
  254.0 18.1 %collective-permute-start = (bf16[512,128]{0,1:T(8,128)(2,1)}, bf16[512,128]{0,1:T(8,128)(2,1)S(1)}, u32[]{:S(2)}, u32[]{:S(2)}) collective-permute-start(bf16[512,128]{0,1:T(8,128)(2,1)} %copy.187), channel_id=1, source_target_pairs={{4,0},{8,4},{12,8},{16,12},{20,16},{24,20},{28,24},{0,28},{5,1},{9... | collective-permute-start | bytes 393224 | tf_op jit(solution)/shard_map/while/body/eval_jaxpr/ppermute | solution.py:20
  257.5 14.6 %collective-permute-start.1 = (bf16[512,128]{1,0:T(8,128)(2,1)}, bf16[512,128]{1,0:T(8,128)(2,1)}, u32[]{:S(2)}, u32[]{:S(2)}) collective-permute-start(bf16[512,128]{1,0:T(8,128)(2,1)} %copy.188), channel_id=1, source_target_pairs={{4,0},{8,4},{12,8},{16,12},{20,16},{24,20},{28,24},{0,28},{5,1},{9... | collective-permute-start | bytes 393224 | tf_op jit(solution)/shard_map/while/body/eval_jaxpr/ppermute | solution.py:20
  263.0 9.0 %collective-permute-start.3 = (f32[512,128]{1,0:T(8,128)}, f32[512,128]{1,0:T(8,128)S(1)}, u32[]{:S(2)}, u32[]{:S(2)}) collective-permute-start(f32[512,128]{1,0:T(8,128)} %add.386), channel_id=1, source_target_pairs={{4,0},{8,4},{12,8},{16,12},{20,16},{24,20},{28,24},{0,28},{5,1},{9... | collective-permute-start | bytes 786440 | tf_op jit(solution)/shard_map/while/body/eval_jaxpr/ppermute | solution.py:20
  267.6 5.3 %collective-permute-start.2 = (f32[512,128]{1,0:T(8,128)}, f32[512,128]{1,0:T(8,128)}, u32[]{:S(2)}, u32[]{:S(2)}) collective-permute-start(f32[512,128]{1,0:T(8,128)} %add.385), channel_id=1, source_target_pairs={{4,0},{8,4},{12,8},{16,12},{20,16},{24,20},{28,24},{0,28},{5,1},{9... | collective-permute-start | bytes 786440 | tf_op jit(solution)/shard_map/while/body/eval_jaxpr/ppermute | solution.py:20
  273.5 17.7 %collective-permute-start = (bf16[512,128]{0,1:T(8,128)(2,1)}, bf16[512,128]{0,1:T(8,128)(2,1)S(1)}, u32[]{:S(2)}, u32[]{:S(2)}) collective-permute-start(bf16[512,128]{0,1:T(8,128)(2,1)} %copy.187), channel_id=1, source_target_pairs={{4,0},{8,4},{12,8},{16,12},{20,16},{24,20},{28,24},{0,28},{5,1},{9... | collective-permute-start | bytes 393224 | tf_op jit(solution)/shard_map/while/body/eval_jaxpr/ppermute | solution.py:20
  277.0 14.2 %collective-permute-start.1 = (bf16[512,128]{1,0:T(8,128)(2,1)}, bf16[512,128]{1,0:T(8,128)(2,1)}, u32[]{:S(2)}, u32[]{:S(2)}) collective-permute-start(bf16[512,128]{1,0:T(8,128)(2,1)} %copy.188), channel_id=1, source_target_pairs={{4,0},{8,4},{12,8},{16,12},{20,16},{24,20},{28,24},{0,28},{5,1},{9... | collective-permute-start | bytes 393224 | tf_op jit(solution)/shard_map/while/body/eval_jaxpr/ppermute | solution.py:20
  283.2 8.0 %collective-permute-start.3 = (f32[512,128]{1,0:T(8,128)}, f32[512,128]{1,0:T(8,128)S(1)}, u32[]{:S(2)}, u32[]{:S(2)}) collective-permute-start(f32[512,128]{1,0:T(8,128)} %add.386), channel_id=1, source_target_pairs={{4,0},{8,4},{12,8},{16,12},{20,16},{24,20},{28,24},{0,28},{5,1},{9... | collective-permute-start | bytes 786440 | tf_op jit(solution)/shard_map/while/body/eval_jaxpr/ppermute | solution.py:20
  287.8 5.3 %collective-permute-start.2 = (f32[512,128]{1,0:T(8,128)}, f32[512,128]{1,0:T(8,128)}, u32[]{:S(2)}, u32[]{:S(2)}) collective-permute-start(f32[512,128]{1,0:T(8,128)} %add.385), channel_id=1, source_target_pairs={{4,0},{8,4},{12,8},{16,12},{20,16},{24,20},{28,24},{0,28},{5,1},{9... | collective-permute-start | bytes 786440 | tf_op jit(solution)/shard_map/while/body/eval_jaxpr/ppermute | solution.py:20
  293.7 27.0 %collective-permute-start = (bf16[512,128]{0,1:T(8,128)(2,1)}, bf16[512,128]{0,1:T(8,128)(2,1)S(1)}, u32[]{:S(2)}, u32[]{:S(2)}) collective-permute-start(bf16[512,128]{0,1:T(8,128)(2,1)} %copy.187), channel_id=1, source_target_pairs={{4,0},{8,4},{12,8},{16,12},{20,16},{24,20},{28,24},{0,28},{5,1},{9... | collective-permute-start | bytes 393224 | tf_op jit(solution)/shard_map/while/body/eval_jaxpr/ppermute | solution.py:20
  297.1 23.5 %collective-permute-start.1 = (bf16[512,128]{1,0:T(8,128)(2,1)}, bf16[512,128]{1,0:T(8,128)(2,1)}, u32[]{:S(2)}, u32[]{:S(2)}) collective-permute-start(bf16[512,128]{1,0:T(8,128)(2,1)} %copy.188), channel_id=1, source_target_pairs={{4,0},{8,4},{12,8},{16,12},{20,16},{24,20},{28,24},{0,28},{5,1},{9... | collective-permute-start | bytes 393224 | tf_op jit(solution)/shard_map/while/body/eval_jaxpr/ppermute | solution.py:20
  302.3 18.3 %collective-permute-start.3 = (f32[512,128]{1,0:T(8,128)}, f32[512,128]{1,0:T(8,128)S(1)}, u32[]{:S(2)}, u32[]{:S(2)}) collective-permute-start(f32[512,128]{1,0:T(8,128)} %add.386), channel_id=1, source_target_pairs={{4,0},{8,4},{12,8},{16,12},{20,16},{24,20},{28,24},{0,28},{5,1},{9... | collective-permute-start | bytes 786440 | tf_op jit(solution)/shard_map/while/body/eval_jaxpr/ppermute | solution.py:20
  317.2 5.3 %collective-permute-start.2 = (f32[512,128]{1,0:T(8,128)}, f32[512,128]{1,0:T(8,128)}, u32[]{:S(2)}, u32[]{:S(2)}) collective-permute-start(f32[512,128]{1,0:T(8,128)} %add.385), channel_id=1, source_target_pairs={{4,0},{8,4},{12,8},{16,12},{20,16},{24,20},{28,24},{0,28},{5,1},{9... | collective-permute-start | bytes 786440 | tf_op jit(solution)/shard_map/while/body/eval_jaxpr/ppermute | solution.py:20
  323.1 26.1 %collective-permute-start = (bf16[512,128]{0,1:T(8,128)(2,1)}, bf16[512,128]{0,1:T(8,128)(2,1)S(1)}, u32[]{:S(2)}, u32[]{:S(2)}) collective-permute-start(bf16[512,128]{0,1:T(8,128)(2,1)} %copy.187), channel_id=1, source_target_pairs={{4,0},{8,4},{12,8},{16,12},{20,16},{24,20},{28,24},{0,28},{5,1},{9... | collective-permute-start | bytes 393224 | tf_op jit(solution)/shard_map/while/body/eval_jaxpr/ppermute | solution.py:20
  326.6 22.6 %collective-permute-start.1 = (bf16[512,128]{1,0:T(8,128)(2,1)}, bf16[512,128]{1,0:T(8,128)(2,1)}, u32[]{:S(2)}, u32[]{:S(2)}) collective-permute-start(bf16[512,128]{1,0:T(8,128)(2,1)} %copy.188), channel_id=1, source_target_pairs={{4,0},{8,4},{12,8},{16,12},{20,16},{24,20},{28,24},{0,28},{5,1},{9... | collective-permute-start | bytes 393224 | tf_op jit(solution)/shard_map/while/body/eval_jaxpr/ppermute | solution.py:20
  331.8 17.4 %collective-permute-start.3 = (f32[512,128]{1,0:T(8,128)}, f32[512,128]{1,0:T(8,128)S(1)}, u32[]{:S(2)}, u32[]{:S(2)}) collective-permute-start(f32[512,128]{1,0:T(8,128)} %add.386), channel_id=1, source_target_pairs={{4,0},{8,4},{12,8},{16,12},{20,16},{24,20},{28,24},{0,28},{5,1},{9... | collective-permute-start | bytes 786440 | tf_op jit(solution)/shard_map/while/body/eval_jaxpr/ppermute | solution.py:20
  345.8 5.3 %collective-permute-start.2 = (f32[512,128]{1,0:T(8,128)}, f32[512,128]{1,0:T(8,128)}, u32[]{:S(2)}, u32[]{:S(2)}) collective-permute-start(f32[512,128]{1,0:T(8,128)} %add.385), channel_id=1, source_target_pairs={{4,0},{8,4},{12,8},{16,12},{20,16},{24,20},{28,24},{0,28},{5,1},{9... | collective-permute-start | bytes 786440 | tf_op jit(solution)/shard_map/while/body/eval_jaxpr/ppermute | solution.py:20
  351.7 26.1 %collective-permute-start = (bf16[512,128]{0,1:T(8,128)(2,1)}, bf16[512,128]{0,1:T(8,128)(2,1)S(1)}, u32[]{:S(2)}, u32[]{:S(2)}) collective-permute-start(bf16[512,128]{0,1:T(8,128)(2,1)} %copy.187), channel_id=1, source_target_pairs={{4,0},{8,4},{12,8},{16,12},{20,16},{24,20},{28,24},{0,28},{5,1},{9... | collective-permute-start | bytes 393224 | tf_op jit(solution)/shard_map/while/body/eval_jaxpr/ppermute | solution.py:20
  355.2 22.6 %collective-permute-start.1 = (bf16[512,128]{1,0:T(8,128)(2,1)}, bf16[512,128]{1,0:T(8,128)(2,1)}, u32[]{:S(2)}, u32[]{:S(2)}) collective-permute-start(bf16[512,128]{1,0:T(8,128)(2,1)} %copy.188), channel_id=1, source_target_pairs={{4,0},{8,4},{12,8},{16,12},{20,16},{24,20},{28,24},{0,28},{5,1},{9... | collective-permute-start | bytes 393224 | tf_op jit(solution)/shard_map/while/body/eval_jaxpr/ppermute | solution.py:20
  360.3 17.5 %collective-permute-start.3 = (f32[512,128]{1,0:T(8,128)}, f32[512,128]{1,0:T(8,128)S(1)}, u32[]{:S(2)}, u32[]{:S(2)}) collective-permute-start(f32[512,128]{1,0:T(8,128)} %add.386), channel_id=1, source_target_pairs={{4,0},{8,4},{12,8},{16,12},{20,16},{24,20},{28,24},{0,28},{5,1},{9... | collective-permute-start | bytes 786440 | tf_op jit(solution)/shard_map/while/body/eval_jaxpr/ppermute | solution.py:20
  374.3 5.3 %collective-permute-start.2 = (f32[512,128]{1,0:T(8,128)}, f32[512,128]{1,0:T(8,128)}, u32[]{:S(2)}, u32[]{:S(2)}) collective-permute-start(f32[512,128]{1,0:T(8,128)} %add.385), channel_id=1, source_target_pairs={{4,0},{8,4},{12,8},{16,12},{20,16},{24,20},{28,24},{0,28},{5,1},{9... | collective-permute-start | bytes 786440 | tf_op jit(solution)/shard_map/while/body/eval_jaxpr/ppermute | solution.py:20
  379.6 39.7 %copy-start.2 = (f32[512,1024]{0,1:T(8,128)S(1)}, f32[512,1024]{0,1:T(8,128)}, u32[]{:S(2)}) copy-start(f32[512,1024]{0,1:T(8,128)} %get-tuple-element.673) | copy-start | bytes 6291460
  396.3 58.0 %copy-start.1 = (bf16[128,512]{1,0:T(8,128)(2,1)S(1)}, bf16[128,512]{1,0:T(8,128)(2,1)}, u32[]{:S(2)}) copy-start(bf16[128,512]{1,0:T(8,128)(2,1)} %param.21) | copy-start | bytes 393220
  397.4 12.3 %collective-permute-start.8 = (f32[512,128]{1,0:T(8,128)S(1)}, f32[512,128]{1,0:T(8,128)S(1)}, u32[]{:S(2)}, u32[]{:S(2)}) collective-permute-start(f32[512,128]{1,0:T(8,128)S(1)} %add.330), channel_id=1, source_target_pairs={{4,0},{8,4},{12,8},{16,12},{20,16},{24,20},{28,24},{0,28},{5,1},{9... | collective-permute-start | bytes 786440 | tf_op jit(solution)/shard_map/ppermute | solution.py:20
  400.6 4.3 collective-permute-start.9
  405.0 11.0 %all-to-all-start.7 = ((bf16[4,128,128]{2,1,0:T(8,128)(2,1)}), bf16[4,128,128]{2,1,0:T(8,128)(2,1)S(1)}, u32[]{:S(2)}, u32[]{:S(2)}) async-start(bf16[4,128,128]{2,1,0:T(8,128)(2,1)} %bitcast.98), calls=%async_computation.7 | async-start | bytes 262144 | tf_op jit(solution)/shard_map/all_to_all | solution.py:178
  416.0 9.2 %all-to-all-start.6 = ((bf16[4,128,128]{2,1,0:T(8,128)(2,1)}), bf16[4,128,128]{2,1,0:T(8,128)(2,1)S(1)}, u32[]{:S(2)}, u32[]{:S(2)}) async-start(bf16[4,128,128]{2,1,0:T(8,128)(2,1)} %bitcast.95), calls=%async_computation.6 | async-start | bytes 262144 | tf_op jit(solution)/shard_map/all_to_all | solution.py:177
  425.2 27.2 %all-to-all-start.5 = ((bf16[4,128,1024]{2,1,0:T(8,128)(2,1)}), bf16[4,128,1024]{2,1,0:T(8,128)(2,1)S(1)}, u32[]{:S(2)}, u32[]{:S(2)}) async-start(bf16[4,128,1024]{2,1,0:T(8,128)(2,1)} %bitcast.92), calls=%async_computation.5 | async-start | bytes 2097152 | tf_op jit(solution)/shard_map/all_to_all | solution.py:176
  (19 other events, 105.5 us)
where the time goes:
time: 457 us; the launch traced here: 454 us
  starting transfers between devices  118 us (26%)
  waiting for transfers between devices  97.4 us (21%)
  blocking collectives  75.4 us (16%)
  other arithmetic  60.2 us (13%)
  local copies, waits for them, and re-layouts  56.1 us (12%)
  matrix products  30.8 us (7%)
  loops' own time  9.46 us (2%)
  between operations  7.61 us (2%)
    ppermute x30, starting transfers between devices, passed_along(): return lax.ppermute(block, axis, route)  78.3 us
    all_gather x1, blocking collectives, per_device(): all_segments = lax.all_gather(doc_ids, ('blk', 'head'), axis=0, tiled=True)  75.4 us
    all_to_all x1, waiting for transfers between devices, per_device(): lax.all_to_all(output_cotangent, 'head', split_axis=1, concat_axis=0, til...  24.1 us
    add x7, other arithmetic, turn_step(): query_total + query_part  22.4 us
    all_to_all x1, waiting for transfers between devices, per_device(): lax.all_to_all(query_matrix, 'head', split_axis=1, concat_axis=0, tiled=T...  22.1 us
    all_to_all x1, waiting for transfers between devices, per_device(): lax.all_to_all(query_grad, 'head', split_axis=0, concat_axis=1, tiled=True)  21.9 us
    ppermute x30, waiting for transfers between devices, passed_along(): return lax.ppermute(block, axis, route)  17.5 us
    while x28, local copies, waits for them, and re-layouts  15.6 us
  transfers between devices with their start and end apart: 42, of which 15 were waited for; matrix products, arithmetic and copies ran while one was open for 26% of the time, Pallas kernels for 0%

commit v1 on v0

--- a/solution.py
+++ b/solution.py
@@ -6,6 +6,24 @@
 HEAD_WIDTH = 128
 DOC_SPAN = 4
 masked_score = -1e30
+
+
+def in_order(tiles, dim):
+    lengths = list(tiles.shape[1:])
+    lengths[dim] *= tiles.shape[0]
+    return jnp.moveaxis(tiles, 0, dim).reshape(lengths)
+
+
+def collected_by_bits(value, axis):
+    size = lax.axis_size(axis)
+    tiles = value[None]
+    for level in range(size.bit_length() - 1):
+        bit = 1 << level
+        other = lax.ppermute(tiles, axis, [(i, i ^ bit) for i in range(size)])
+        both = jnp.stack([tiles, other])
+        upper = lax.axis_index(axis) >> level & 1
+        tiles = jnp.where(upper == 0, both, both[::-1]).reshape(-1, *value.shape)
+    return tiles
 
 
 def shifted(block, axis, distance):
@@ -35,7 +53,7 @@
         lax.all_to_all(key_matrix, "head", split_axis=1, concat_axis=0, tiled=True),
         lax.all_to_all(value_matrix, "head", split_axis=1, concat_axis=0, tiled=True),
     )
-    all_segments = lax.all_gather(doc_ids, ("blk", "head"), axis=0, tiled=True)
+    all_segments = in_order(collected_by_bits(doc_ids, ("blk", "head")), 0)
     my_block = lax.axis_index("blk")
     query_tensor = query_local.reshape(block_rows, kv_heads, heads_per_group, HEAD_WIDTH)
     returned_grads = grad_local.reshape(block_rows, kv_heads, heads_per_group, HEAD_WIDTH)

time: 457 us -> 389 us (0.85)
  blocking collectives: 75.4 us -> 0 us
  starting transfers between devices: 118 us -> 123 us
    all_gather x1 -> x0, blocking collectives: 75.4 us -> none  [per_device(): all_segments = lax.all_gather(doc_ids, ('blk', 'head'), axis=0, tiled=True)]
    ppermute x0 -> x5, waiting for transfers between devices: none -> 24.4 us  [collected_by_bits(): other = lax.ppermute(tiles, axis, [(i, i ^ bit) for i in range(size)])]
    all_to_all x1, waiting for transfers between devices: 24.1 us -> 0.01 us  [per_device(): lax.all_to_all(output_cotangent, 'head', split_axis=1, concat_axis=0, til...]
    ppermute x0 -> x5, starting transfers between devices: none -> 7.57 us  [collected_by_bits(): other = lax.ppermute(tiles, axis, [(i, i ^ bit) for i in range(size)])]
  transfers between devices with their start and end apart: 42 -> 47, of which waited for: 15 -> 19; matrix products, arithmetic and copies ran while one was open for 26% -> 31% of each run, Pallas kernels for 0% -> 0%
where the time goes in v1:
time: 389 us; the launch traced here: 386 us
  starting transfers between devices  123 us (32%)
  waiting for transfers between devices  99.1 us (25%)
  other arithmetic  60.2 us (15%)
  local copies, waits for them, and re-layouts  56.2 us (14%)
  matrix products  30.8 us (8%)
  loops' own time  9.43 us (2%)
  between operations  7.41 us (2%)
    ppermute x30, starting transfers between devices, passed_along(): return lax.ppermute(block, axis, route)  77.6 us
    ppermute x5, waiting for transfers between devices, collected_by_bits(): other = lax.ppermute(tiles, axis, [(i, i ^ bit) for i in range(size)])  24.4 us
    add x7, other arithmetic, turn_step(): query_total + query_part  22.5 us
    all_to_all x1, waiting for transfers between devices, per_device(): lax.all_to_all(query_matrix, 'head', split_axis=1, concat_axis=0, tiled=T...  22.1 us
    all_to_all x1, waiting for transfers between devices, per_device(): lax.all_to_all(query_grad, 'head', split_axis=0, concat_axis=1, tiled=True)  21.9 us
    ppermute x30, waiting for transfers between devices, passed_along(): return lax.ppermute(block, axis, route)  17.4 us
    while x28, local copies, waits for them, and re-layouts  15.6 us
    add x7, other arithmetic, turn_step(): summed_key_grad + key_part  12.3 us
  transfers between devices with their start and end apart: 47, of which 19 were waited for; matrix products, arithmetic and copies ran while one was open for 31% of the time, Pallas kernels for 0%

profile of v1, /device:TPU:6, one launch (start us, length us, event | category | flops | bytes accessed | tf_op | source)
XLA Modules:
  0.0 385.9 jit_solution(15656317097572810317)
XLA Ops:
  2.2 4.9 %all-to-all-start = ((bf16[128,4,128]{2,0,1:T(8,128)(2,1)}), bf16[128,4,128]{2,0,1:T(8,128)(2,1)}, u32[]{:S(2)}, u32[]{:S(2)}) async-start(bf16[128,4,128]{2,0,1:T(8,128)(2,1)} %copy_bitcast_fusion.4), calls=%async_computation | async-start | bytes 262144 | tf_op jit(solution)/shard_map/all_to_all | solution.py:53
  7.1 2.3 copy.157
  9.4 3.9 %all-to-all-done = bf16[128,4,128]{2,0,1:T(8,128)(2,1)} async-done(((bf16[128,4,128]{2,0,1:T(8,128)(2,1)}), bf16[128,4,128]{2,0,1:T(8,128)(2,1)}, u32[]{:S(2)}, u32[]{:S(2)}) %all-to-all-start) | async-done | bytes 131104 | tf_op jit(solution)/shard_map/all_to_all | solution.py:53
  13.3 3.5 all-to-all-start.2
  16.8 2.3 copy.156
  19.1 22.1 %all-to-all-done.2 = bf16[128,4,1024]{2,0,1:T(8,128)(2,1)S(1)} async-done(((bf16[128,4,1024]{2,0,1:T(8,128)(2,1)}), bf16[128,4,1024]{2,0,1:T(8,128)(2,1)S(1)}, u32[]{:S(2)}, u32[]{:S(2)}) %all-to-all-start.2) | async-done | bytes 1048608 | tf_op jit(solution)/shard_map/all_to_all | solution.py:50
  41.2 3.5 all-to-all-start.3
  46.7 14.6 %collective-permute-done.4 = s32[1,128]{1,0:T(1,128)S(1)} collective-permute-done((s32[1,128]{1,0:T(1,128)S(1)}, s32[1,128]{1,0:T(1,128)S(1)}, u32[]{:S(2)}, u32[]{:S(2)}) %collective-permute-start.4) | collective-permute-done | bytes 544 | tf_op jit(solution)/shard_map/ppermute | solution.py:22
  61.4 4.5 %collective-permute-start.5 = (s32[2,128]{1,0:T(2,128)S(1)}, s32[2,128]{1,0:T(2,128)S(1)}, u32[]{:S(2)}, u32[]{:S(2)}) collective-permute-start(s32[2,128]{1,0:T(2,128)S(1)} %bitcast.390), channel_id=1, source_target_pairs={{0,2},{1,3},{2,0},{3,1},{4,6},{5,7},{6,4},{7,5},{8,10},{9,11},{10,... | collective-permute-start | bytes 3080 | tf_op jit(solution)/shard_map/ppermute | solution.py:22
  65.9 4.1 %collective-permute-done.5 = s32[2,128]{1,0:T(2,128)S(1)} collective-permute-done((s32[2,128]{1,0:T(2,128)S(1)}, s32[2,128]{1,0:T(2,128)S(1)}, u32[]{:S(2)}, u32[]{:S(2)}) %collective-permute-start.5) | collective-permute-done | bytes 1056 | tf_op jit(solution)/shard_map/ppermute | solution.py:22
  71.2 4.3 %all-to-all-start.4 = ((bf16[128,4,1024]{2,0,1:T(8,128)(2,1)}), bf16[128,4,1024]{2,0,1:T(8,128)(2,1)}, u32[]{:S(2)}, u32[]{:S(2)}) async-start(bf16[128,4,1024]{2,0,1:T(8,128)(2,1)} %bitcast.340), calls=%async_computation.4 | async-start | bytes 2097152 | tf_op jit(solution)/shard_map/all_to_all | solution.py:52
  76.7 2.4 collective-permute-done.7
  79.7 3.1 collective-permute-done.8
  102.1 3.9 %all-to-all-start.1 = ((bf16[128,4,128]{2,0,1:T(8,128)(2,1)}), bf16[128,4,128]{2,0,1:T(8,128)(2,1)}, u32[]{:S(2)}, u32[]{:S(2)}) async-start(bf16[128,4,128]{2,0,1:T(8,128)(2,1)} %copy_bitcast_fusion.3), calls=%async_computation.1 | async-start | bytes 262144 | tf_op jit(solution)/shard_map/all_to_all | solution.py:54
  111.1 2.5 fusion.78
  115.7 5.7 %conditional.6 = ((f32[1,8,512,1]{2,1,3,0:T(8,128)S(1)}, f32[1,8,512,1]{2,1,3,0:T(8,128)S(1)})) conditional(s32[]{:T(128)} %convert_element_type.80, (f32[1,8,512,1]{2,1,3,0:T(8,128)S(1)}, f32[1,8,512,1]{2,1,3,0:T(8,128)S(1)}) %tuple.89, (s32[512]{0:T(512)S(1)}, s32[]{:T(128)}, s32[4096]{0:T(1024)}, s32[512]{0:T(512)S(1)}, ...), branch_computations={%region_2.3_spmd, %region_3.6_spmd} | conditional | flops 554443264 | bytes 18970726 | solution.py:108
  116.7 2.5 fusion.2
  123.9 187.3 %while.26 = (s32[]{:T(128)}, bf16[512,128]{0,1:T(8,128)(2,1)S(1)}, bf16[512,128]{1,0:T(8,128)(2,1)}, f32[512,1024]{0,1:T(8,128)}, f32[512,128]{1,0:T(8,128)}, /*...) while((s32[]{:T(128)}, bf16[512,128]{0,1:T(8,128)(2,1)S(1)}, ...), condition=%wide.region_22.23_spmd.clone, body=%wide.region_19.22_spmd.clone.sunk | while | flops 2711487488 | bytes 62722972 | solution.py:181
  124.5 17.9 %collective-permute-start = (bf16[512,128]{0,1:T(8,128)(2,1)}, bf16[512,128]{0,1:T(8,128)(2,1)S(1)}, u32[]{:S(2)}, u32[]{:S(2)}) collective-permute-start(bf16[512,128]{0,1:T(8,128)(2,1)} %copy.187), channel_id=1, source_target_pairs={{4,0},{8,4},{12,8},{16,12},{20,16},{24,20},{28,24},{0,28},{5,1},{9... | collective-permute-start | bytes 393224 | tf_op jit(solution)/shard_map/while/body/eval_jaxpr/ppermute | solution.py:38
  146.4 13.3 %conditional.13 = (f32[512,1024]{0,1:T(8,128)S(1)}, f32[512,128]{1,0:T(8,128)}, f32[512,128]{1,0:T(8,128)S(1)}) conditional(s32[]{:T(128)} %convert_element_type.114, () %tuple.153, (s32[512]{0:T(512)S(1)}, s32[]{:T(128)}, s32[4096]{0:T(1024)}, s32[]{:T(128)}, bf16[512,1,8,128]{3,0,2,1:T(8,128)(2,1)S(1)}, /*index=5*/bf16[512,128]{0,1:T(8,128)(2,1)}, ...), branch_computations={%region_20.20_spmd, %region_21.21_spmd} | conditional | flops 2710307840 | bytes 50137280 | solution.py:151
  147.6 2.2 fusion.39
  149.8 2.1 fusion.33
  151.9 4.2 %fusion.29 = bf16[8,512,512]{1,2,0:T(8,128)(2,1)S(1)} fusion(f32[512,512,8]{1,0,2:T(8,128)S(1)} %fusion.39, f32[8,512]{1,0:T(8,128)S(1)} %bitcast.379, f32[8,512]{1,0:T(8,128)S(1)} %bitcast.381, pred[512,512]{0,1:T(8,128)(4,1)S(1)} %compare_and_fusion.4, bf16[512,1,8,128]{3,0,2,1:T(8,128)(2,1)S(1)} %copy-done.11, bf16[512,128]{1,0:T(8,128)(2,1)} %get-tuple-element.614), kind=kOutput, calls=%fused_computation.54 | convolution fusion | flops 551550976 | bytes 14057472 | tf_op jit(solution)/shard_map/while/body/eval_jaxpr/cond/branch_1_fun/ighd,jgd->ghij/dot_general | solution.py:123
  165.6 2.8 collective-permute-done.2
  179.5 3.4 select_add_fusion.2
  194.5 2.8 collective-permute-start.3
  200.2 3.4 select_add_fusion.2
  214.7 2.8 collective-permute-start.3
  219.3 3.4 select_add_fusion.2
  233.8 13.2 %collective-permute-start.3 = (f32[512,128]{1,0:T(8,128)}, f32[512,128]{1,0:T(8,128)S(1)}, u32[]{:S(2)}, u32[]{:S(2)}) collective-permute-start(f32[512,128]{1,0:T(8,128)} %add.404), channel_id=1, source_target_pairs={{4,0},{8,4},{12,8},{16,12},{20,16},{24,20},{28,24},{0,28},{5,1},{9... | collective-permute-start | bytes 786440 | tf_op jit(solution)/shard_map/while/body/eval_jaxpr/ppermute | solution.py:38
  248.7 3.4 select_add_fusion.2
  263.3 12.3 %collective-permute-start.3 = (f32[512,128]{1,0:T(8,128)}, f32[512,128]{1,0:T(8,128)S(1)}, u32[]{:S(2)}, u32[]{:S(2)}) collective-permute-start(f32[512,128]{1,0:T(8,128)} %add.404), channel_id=1, source_target_pairs={{4,0},{8,4},{12,8},{16,12},{20,16},{24,20},{28,24},{0,28},{5,1},{9... | collective-permute-start | bytes 786440 | tf_op jit(solution)/shard_map/while/body/eval_jaxpr/ppermute | solution.py:38
  277.3 3.4 select_add_fusion.2
  291.9 12.3 %collective-permute-start.3 = (f32[512,128]{1,0:T(8,128)}, f32[512,128]{1,0:T(8,128)S(1)}, u32[]{:S(2)}, u32[]{:S(2)}) collective-permute-start(f32[512,128]{1,0:T(8,128)} %add.404), channel_id=1, source_target_pairs={{4,0},{8,4},{12,8},{16,12},{20,16},{24,20},{28,24},{0,28},{5,1},{9... | collective-permute-start | bytes 786440 | tf_op jit(solution)/shard_map/while/body/eval_jaxpr/ppermute | solution.py:38
  305.9 3.4 select_add_fusion.2
  311.1 16.7 %conditional.10 = (f32[512,1024]{0,1:T(8,128)}, f32[512,128]{1,0:T(8,128)}, f32[512,128]{1,0:T(8,128)}) conditional(s32[]{:T(128)} %convert_element_type.85, () %tuple.95, (s32[512]{0:T(512)S(1)}, s32[]{:T(128)}, s32[4096]{0:T(1024)}, s32[512]{0:T(512)S(1)}, bf16[512,1,8,128]{3,2,0,1:T(8,128)(2,1)}, /*index=5*/bf16[512,128]{0,1:T(8,128)(2,1)S(1)}, ...), branch_computations={%region_23.24_spmd, %region_24.25_spmd} | conditional | flops 2710307328 | bytes 54360276 | solution.py:151
  314.0 2.5 fusion.65
  316.6 2.9 fusion.59
  319.4 4.4 %fusion.55 = bf16[8,512,512]{1,2,0:T(8,128)(2,1)S(1)} fusion(f32[512,512,8]{1,0,2:T(8,128)S(1)} %fusion.65, f32[8,512]{1,0:T(8,128)S(1)} %bitcast.384, f32[8,512]{1,0:T(8,128)S(1)} %bitcast.383, pred[512,512]{0,1:T(8,128)(4,1)S(1)} %compare_and_fusion.5, bf16[512,1,8,128]{3,2,0,1:T(8,128)(2,1)S(1)} %copy-done.8, bf16[512,128]{1,0:T(8,128)(2,1)} %get-tuple-element.643), kind=kOutput, calls=%fused_computation.83 | convolution fusion | flops 551550976 | bytes 14057472 | tf_op jit(solution)/shard_map/cond/branch_1_fun/ighd,jgd->ghij/dot_general | solution.py:123
  329.0 2.2 collective-permute-start.13
  332.3 4.2 %collective-permute-done.14 = bf16[512,128]{1,0:T(8,128)(2,1)} collective-permute-done((bf16[512,128]{1,0:T(8,128)(2,1)S(1)}, bf16[512,128]{1,0:T(8,128)(2,1)}, u32[]{:S(2)}, u32[]{:S(2)}) %collective-permute-start.14) | collective-permute-done | bytes 131104 | tf_op jit(solution)/shard_map/ppermute | solution.py:38
  336.5 4.8 %all-to-all-start.7 = ((bf16[4,128,128]{2,1,0:T(8,128)(2,1)}), bf16[4,128,128]{2,1,0:T(8,128)(2,1)S(1)}, u32[]{:S(2)}, u32[]{:S(2)}) async-start(bf16[4,128,128]{2,1,0:T(8,128)(2,1)} %bitcast.112), calls=%async_computation.7 | async-start | bytes 262144 | tf_op jit(solution)/shard_map/all_to_all | solution.py:196
  342.0 5.5 %all-to-all-done.7 = bf16[4,128,128]{2,1,0:T(8,128)(2,1)S(1)} async-done(((bf16[4,128,128]{2,1,0:T(8,128)(2,1)}), bf16[4,128,128]{2,1,0:T(8,128)(2,1)S(1)}, u32[]{:S(2)}, u32[]{:S(2)}) %all-to-all-start.7) | async-done | bytes 131104 | tf_op jit(solution)/shard_map/all_to_all | solution.py:196
  347.5 3.3 all-to-all-start.6
  350.8 2.1 multiply_convert_fusion
  354.3 2.4 all-to-all-done.6
  356.7 3.5 all-to-all-start.5
  362.1 21.9 %all-to-all-done.5 = bf16[4,128,1024]{2,1,0:T(8,128)(2,1)S(1)} async-done(((bf16[4,128,1024]{2,1,0:T(8,128)(2,1)}), bf16[4,128,1024]{2,1,0:T(8,128)(2,1)S(1)}, u32[]{:S(2)}, u32[]{:S(2)}) %all-to-all-start.5) | async-done | bytes 1048608 | tf_op jit(solution)/shard_map/all_to_all | solution.py:194
  (248 shorter events, 138.3 us)
Async XLA Ops:
  1.5 74.5 %copy-start.12 = (bf16[128,512]{1,0:T(8,128)(2,1)S(1)}, bf16[128,512]{1,0:T(8,128)(2,1)}, u32[]{:S(2)}) copy-start(bf16[128,512]{1,0:T(8,128)(2,1)} %param.22) | copy-start | bytes 393220
  2.2 11.1 %all-to-all-start = ((bf16[128,4,128]{2,0,1:T(8,128)(2,1)}), bf16[128,4,128]{2,0,1:T(8,128)(2,1)}, u32[]{:S(2)}, u32[]{:S(2)}) async-start(bf16[128,4,128]{2,0,1:T(8,128)(2,1)} %copy_bitcast_fusion.4), calls=%async_computation | async-start | bytes 262144 | tf_op jit(solution)/shard_map/all_to_all | solution.py:53
  13.3 28.0 %all-to-all-start.2 = ((bf16[128,4,1024]{2,0,1:T(8,128)(2,1)}), bf16[128,4,1024]{2,0,1:T(8,128)(2,1)S(1)}, u32[]{:S(2)}, u32[]{:S(2)}) async-start(bf16[128,4,1024]{2,0,1:T(8,128)(2,1)} %bitcast.342), calls=%async_computation.2 | async-start | bytes 2097152 | tf_op jit(solution)/shard_map/all_to_all | solution.py:50
  41.2 30.0 %all-to-all-start.3 = ((bf16[128,4,1024]{2,0,1:T(8,128)(2,1)}), bf16[128,4,1024]{2,0,1:T(8,128)(2,1)S(1)}, u32[]{:S(2)}, u32[]{:S(2)}) async-start(bf16[128,4,1024]{2,0,1:T(8,128)(2,1)} %bitcast.341), calls=%async_computation.3 | async-start | bytes 2097152 | tf_op jit(solution)/shard_map/all_to_all | solution.py:51
  44.8 16.6 %collective-permute-start.4 = (s32[1,128]{1,0:T(1,128)S(1)}, s32[1,128]{1,0:T(1,128)S(1)}, u32[]{:S(2)}, u32[]{:S(2)}) collective-permute-start(s32[1,128]{1,0:T(1,128)S(1)} %bitcast.395), channel_id=1, source_target_pairs={{0,1},{1,0},{2,3},{3,2},{4,5},{5,4},{6,7},{7,6},{8,9},{9,8},{10,11... | collective-permute-start | bytes 1544 | tf_op jit(solution)/shard_map/ppermute | solution.py:22
  61.4 8.6 %collective-permute-start.5 = (s32[2,128]{1,0:T(2,128)S(1)}, s32[2,128]{1,0:T(2,128)S(1)}, u32[]{:S(2)}, u32[]{:S(2)}) collective-permute-start(s32[2,128]{1,0:T(2,128)S(1)} %bitcast.390), channel_id=1, source_target_pairs={{0,2},{1,3},{2,0},{3,1},{4,6},{5,7},{6,4},{7,5},{8,10},{9,11},{10,... | collective-permute-start | bytes 3080 | tf_op jit(solution)/shard_map/ppermute | solution.py:22
  70.0 1.2 collective-permute-start.6
  71.2 31.0 %all-to-all-start.4 = ((bf16[128,4,1024]{2,0,1:T(8,128)(2,1)}), bf16[128,4,1024]{2,0,1:T(8,128)(2,1)}, u32[]{:S(2)}, u32[]{:S(2)}) async-start(bf16[128,4,1024]{2,0,1:T(8,128)(2,1)} %bitcast.340), calls=%async_computation.4 | async-start | bytes 2097152 | tf_op jit(solution)/shard_map/all_to_all | solution.py:52
  75.5 3.7 collective-permute-start.7
  79.2 3.7 collective-permute-start.8
  91.3 30.3 %collective-permute-start.12 = (bf16[512,128]{1,0:T(8,128)(2,1)}, bf16[512,128]{1,0:T(8,128)(2,1)}, u32[]{:S(2)}, u32[]{:S(2)}) collective-permute-start(bf16[512,128]{1,0:T(8,128)(2,1)} %bitcast.67), channel_id=1, source_target_pairs={{0,16},{4,20},{8,24},{12,28},{1,17},{5,21},{9,25},{13,29},{2,18},{... | collective-permute-start | bytes 393224 | tf_op jit(solution)/shard_map/ppermute | solution.py:32
  92.6 28.9 %collective-permute-start.11 = (bf16[512,128]{1,0:T(8,128)(2,1)}, bf16[512,128]{1,0:T(8,128)(2,1)}, u32[]{:S(2)}, u32[]{:S(2)}) collective-permute-start(bf16[512,128]{1,0:T(8,128)(2,1)} %bitcast.67), channel_id=1, source_target_pairs={{0,12},{4,16},{8,20},{12,24},{16,28},{1,13},{5,17},{9,21},{13,25},... | collective-permute-start | bytes 393224 | tf_op jit(solution)/shard_map/ppermute | solution.py:32
  93.9 27.4 %collective-permute-start.10 = (bf16[512,128]{1,0:T(8,128)(2,1)}, bf16[512,128]{1,0:T(8,128)(2,1)}, u32[]{:S(2)}, u32[]{:S(2)}) collective-permute-start(bf16[512,128]{1,0:T(8,128)(2,1)} %bitcast.67), channel_id=1, source_target_pairs={{0,8},{4,12},{8,16},{12,20},{16,24},{20,28},{1,9},{5,13},{9,17},{1... | collective-permute-start | bytes 393224 | tf_op jit(solution)/shard_map/ppermute | solution.py:32
  95.2 20.5 %collective-permute-start.9 = (bf16[512,128]{1,0:T(8,128)(2,1)}, bf16[512,128]{1,0:T(8,128)(2,1)}, u32[]{:S(2)}, u32[]{:S(2)}) collective-permute-start(bf16[512,128]{1,0:T(8,128)(2,1)} %bitcast.67), channel_id=1, source_target_pairs={{0,4},{4,8},{8,12},{12,16},{16,20},{20,24},{24,28},{1,5},{5,9},{9,... | collective-permute-start | bytes 393224 | tf_op jit(solution)/shard_map/ppermute | solution.py:32
  102.1 20.3 %all-to-all-start.1 = ((bf16[128,4,128]{2,0,1:T(8,128)(2,1)}), bf16[128,4,128]{2,0,1:T(8,128)(2,1)}, u32[]{:S(2)}, u32[]{:S(2)}) async-start(bf16[128,4,128]{2,0,1:T(8,128)(2,1)} %copy_bitcast_fusion.3), calls=%async_computation.1 | async-start | bytes 262144 | tf_op jit(solution)/shard_map/all_to_all | solution.py:54
  124.5 40.5 %collective-permute-start = (bf16[512,128]{0,1:T(8,128)(2,1)}, bf16[512,128]{0,1:T(8,128)(2,1)S(1)}, u32[]{:S(2)}, u32[]{:S(2)}) collective-permute-start(bf16[512,128]{0,1:T(8,128)(2,1)} %copy.187), channel_id=1, source_target_pairs={{4,0},{8,4},{12,8},{16,12},{20,16},{24,20},{28,24},{0,28},{5,1},{9... | collective-permute-start | bytes 393224 | tf_op jit(solution)/shard_map/while/body/eval_jaxpr/ppermute | solution.py:38
  144.0 21.0 %collective-permute-start.1 = (bf16[512,128]{1,0:T(8,128)(2,1)}, bf16[512,128]{1,0:T(8,128)(2,1)}, u32[]{:S(2)}, u32[]{:S(2)}) collective-permute-start(bf16[512,128]{1,0:T(8,128)(2,1)} %copy.188), channel_id=1, source_target_pairs={{4,0},{8,4},{12,8},{16,12},{20,16},{24,20},{28,24},{0,28},{5,1},{9... | collective-permute-start | bytes 393224 | tf_op jit(solution)/shard_map/while/body/eval_jaxpr/ppermute | solution.py:38
  161.4 4.2 %collective-permute-start.3 = (f32[512,128]{1,0:T(8,128)}, f32[512,128]{1,0:T(8,128)S(1)}, u32[]{:S(2)}, u32[]{:S(2)}) collective-permute-start(f32[512,128]{1,0:T(8,128)} %add.404), channel_id=1, source_target_pairs={{4,0},{8,4},{12,8},{16,12},{20,16},{24,20},{28,24},{0,28},{5,1},{9... | collective-permute-start | bytes 786440 | tf_op jit(solution)/shard_map/while/body/eval_jaxpr/ppermute | solution.py:38
  163.1 5.3 %collective-permute-start.2 = (f32[512,128]{1,0:T(8,128)}, f32[512,128]{1,0:T(8,128)}, u32[]{:S(2)}, u32[]{:S(2)}) collective-permute-start(f32[512,128]{1,0:T(8,128)} %add.403), channel_id=1, source_target_pairs={{4,0},{8,4},{12,8},{16,12},{20,16},{24,20},{28,24},{0,28},{5,1},{9... | collective-permute-start | bytes 786440 | tf_op jit(solution)/shard_map/while/body/eval_jaxpr/ppermute | solution.py:38
  169.0 13.8 %collective-permute-start = (bf16[512,128]{0,1:T(8,128)(2,1)}, bf16[512,128]{0,1:T(8,128)(2,1)S(1)}, u32[]{:S(2)}, u32[]{:S(2)}) collective-permute-start(bf16[512,128]{0,1:T(8,128)(2,1)} %copy.187), channel_id=1, source_target_pairs={{4,0},{8,4},{12,8},{16,12},{20,16},{24,20},{28,24},{0,28},{5,1},{9... | collective-permute-start | bytes 393224 | tf_op jit(solution)/shard_map/while/body/eval_jaxpr/ppermute | solution.py:38
  172.5 10.4 %collective-permute-start.1 = (bf16[512,128]{1,0:T(8,128)(2,1)}, bf16[512,128]{1,0:T(8,128)(2,1)}, u32[]{:S(2)}, u32[]{:S(2)}) collective-permute-start(bf16[512,128]{1,0:T(8,128)(2,1)} %copy.188), channel_id=1, source_target_pairs={{4,0},{8,4},{12,8},{16,12},{20,16},{24,20},{28,24},{0,28},{5,1},{9... | collective-permute-start | bytes 393224 | tf_op jit(solution)/shard_map/while/body/eval_jaxpr/ppermute | solution.py:38
  177.7 5.2 %collective-permute-start.3 = (f32[512,128]{1,0:T(8,128)}, f32[512,128]{1,0:T(8,128)S(1)}, u32[]{:S(2)}, u32[]{:S(2)}) collective-permute-start(f32[512,128]{1,0:T(8,128)} %add.404), channel_id=1, source_target_pairs={{4,0},{8,4},{12,8},{16,12},{20,16},{24,20},{28,24},{0,28},{5,1},{9... | collective-permute-start | bytes 786440 | tf_op jit(solution)/shard_map/while/body/eval_jaxpr/ppermute | solution.py:38
  179.5 5.3 %collective-permute-start.2 = (f32[512,128]{1,0:T(8,128)}, f32[512,128]{1,0:T(8,128)}, u32[]{:S(2)}, u32[]{:S(2)}) collective-permute-start(f32[512,128]{1,0:T(8,128)} %add.403), channel_id=1, source_target_pairs={{4,0},{8,4},{12,8},{16,12},{20,16},{24,20},{28,24},{0,28},{5,1},{9... | collective-permute-start | bytes 786440 | tf_op jit(solution)/shard_map/while/body/eval_jaxpr/ppermute | solution.py:38
  185.4 18.2 %collective-permute-start = (bf16[512,128]{0,1:T(8,128)(2,1)}, bf16[512,128]{0,1:T(8,128)(2,1)S(1)}, u32[]{:S(2)}, u32[]{:S(2)}) collective-permute-start(bf16[512,128]{0,1:T(8,128)(2,1)} %copy.187), channel_id=1, source_target_pairs={{4,0},{8,4},{12,8},{16,12},{20,16},{24,20},{28,24},{0,28},{5,1},{9... | collective-permute-start | bytes 393224 | tf_op jit(solution)/shard_map/while/body/eval_jaxpr/ppermute | solution.py:38
  188.8 14.8 %collective-permute-start.1 = (bf16[512,128]{1,0:T(8,128)(2,1)}, bf16[512,128]{1,0:T(8,128)(2,1)}, u32[]{:S(2)}, u32[]{:S(2)}) collective-permute-start(bf16[512,128]{1,0:T(8,128)(2,1)} %copy.188), channel_id=1, source_target_pairs={{4,0},{8,4},{12,8},{16,12},{20,16},{24,20},{28,24},{0,28},{5,1},{9... | collective-permute-start | bytes 393224 | tf_op jit(solution)/shard_map/while/body/eval_jaxpr/ppermute | solution.py:38
  194.5 9.1 %collective-permute-start.3 = (f32[512,128]{1,0:T(8,128)}, f32[512,128]{1,0:T(8,128)S(1)}, u32[]{:S(2)}, u32[]{:S(2)}) collective-permute-start(f32[512,128]{1,0:T(8,128)} %add.404), channel_id=1, source_target_pairs={{4,0},{8,4},{12,8},{16,12},{20,16},{24,20},{28,24},{0,28},{5,1},{9... | collective-permute-start | bytes 786440 | tf_op jit(solution)/shard_map/while/body/eval_jaxpr/ppermute | solution.py:38
  199.1 5.3 %collective-permute-start.2 = (f32[512,128]{1,0:T(8,128)}, f32[512,128]{1,0:T(8,128)}, u32[]{:S(2)}, u32[]{:S(2)}) collective-permute-start(f32[512,128]{1,0:T(8,128)} %add.403), channel_id=1, source_target_pairs={{4,0},{8,4},{12,8},{16,12},{20,16},{24,20},{28,24},{0,28},{5,1},{9... | collective-permute-start | bytes 786440 | tf_op jit(solution)/shard_map/while/body/eval_jaxpr/ppermute | solution.py:38
  205.0 17.7 %collective-permute-start = (bf16[512,128]{0,1:T(8,128)(2,1)}, bf16[512,128]{0,1:T(8,128)(2,1)S(1)}, u32[]{:S(2)}, u32[]{:S(2)}) collective-permute-start(bf16[512,128]{0,1:T(8,128)(2,1)} %copy.187), channel_id=1, source_target_pairs={{4,0},{8,4},{12,8},{16,12},{20,16},{24,20},{28,24},{0,28},{5,1},{9... | collective-permute-start | bytes 393224 | tf_op jit(solution)/shard_map/while/body/eval_jaxpr/ppermute | solution.py:38
  208.5 14.2 %collective-permute-start.1 = (bf16[512,128]{1,0:T(8,128)(2,1)}, bf16[512,128]{1,0:T(8,128)(2,1)}, u32[]{:S(2)}, u32[]{:S(2)}) collective-permute-start(bf16[512,128]{1,0:T(8,128)(2,1)} %copy.188), channel_id=1, source_target_pairs={{4,0},{8,4},{12,8},{16,12},{20,16},{24,20},{28,24},{0,28},{5,1},{9... | collective-permute-start | bytes 393224 | tf_op jit(solution)/shard_map/while/body/eval_jaxpr/ppermute | solution.py:38
  214.7 8.0 %collective-permute-start.3 = (f32[512,128]{1,0:T(8,128)}, f32[512,128]{1,0:T(8,128)S(1)}, u32[]{:S(2)}, u32[]{:S(2)}) collective-permute-start(f32[512,128]{1,0:T(8,128)} %add.404), channel_id=1, source_target_pairs={{4,0},{8,4},{12,8},{16,12},{20,16},{24,20},{28,24},{0,28},{5,1},{9... | collective-permute-start | bytes 786440 | tf_op jit(solution)/shard_map/while/body/eval_jaxpr/ppermute | solution.py:38
  219.3 5.3 %collective-permute-start.2 = (f32[512,128]{1,0:T(8,128)}, f32[512,128]{1,0:T(8,128)}, u32[]{:S(2)}, u32[]{:S(2)}) collective-permute-start(f32[512,128]{1,0:T(8,128)} %add.403), channel_id=1, source_target_pairs={{4,0},{8,4},{12,8},{16,12},{20,16},{24,20},{28,24},{0,28},{5,1},{9... | collective-permute-start | bytes 786440 | tf_op jit(solution)/shard_map/while/body/eval_jaxpr/ppermute | solution.py:38
  225.2 27.0 %collective-permute-start = (bf16[512,128]{0,1:T(8,128)(2,1)}, bf16[512,128]{0,1:T(8,128)(2,1)S(1)}, u32[]{:S(2)}, u32[]{:S(2)}) collective-permute-start(bf16[512,128]{0,1:T(8,128)(2,1)} %copy.187), channel_id=1, source_target_pairs={{4,0},{8,4},{12,8},{16,12},{20,16},{24,20},{28,24},{0,28},{5,1},{9... | collective-permute-start | bytes 393224 | tf_op jit(solution)/shard_map/while/body/eval_jaxpr/ppermute | solution.py:38
  228.7 23.5 %collective-permute-start.1 = (bf16[512,128]{1,0:T(8,128)(2,1)}, bf16[512,128]{1,0:T(8,128)(2,1)}, u32[]{:S(2)}, u32[]{:S(2)}) collective-permute-start(bf16[512,128]{1,0:T(8,128)(2,1)} %copy.188), channel_id=1, source_target_pairs={{4,0},{8,4},{12,8},{16,12},{20,16},{24,20},{28,24},{0,28},{5,1},{9... | collective-permute-start | bytes 393224 | tf_op jit(solution)/shard_map/while/body/eval_jaxpr/ppermute | solution.py:38
  233.8 18.4 %collective-permute-start.3 = (f32[512,128]{1,0:T(8,128)}, f32[512,128]{1,0:T(8,128)S(1)}, u32[]{:S(2)}, u32[]{:S(2)}) collective-permute-start(f32[512,128]{1,0:T(8,128)} %add.404), channel_id=1, source_target_pairs={{4,0},{8,4},{12,8},{16,12},{20,16},{24,20},{28,24},{0,28},{5,1},{9... | collective-permute-start | bytes 786440 | tf_op jit(solution)/shard_map/while/body/eval_jaxpr/ppermute | solution.py:38
  248.7 5.3 %collective-permute-start.2 = (f32[512,128]{1,0:T(8,128)}, f32[512,128]{1,0:T(8,128)}, u32[]{:S(2)}, u32[]{:S(2)}) collective-permute-start(f32[512,128]{1,0:T(8,128)} %add.403), channel_id=1, source_target_pairs={{4,0},{8,4},{12,8},{16,12},{20,16},{24,20},{28,24},{0,28},{5,1},{9... | collective-permute-start | bytes 786440 | tf_op jit(solution)/shard_map/while/body/eval_jaxpr/ppermute | solution.py:38
  254.7 26.1 %collective-permute-start = (bf16[512,128]{0,1:T(8,128)(2,1)}, bf16[512,128]{0,1:T(8,128)(2,1)S(1)}, u32[]{:S(2)}, u32[]{:S(2)}) collective-permute-start(bf16[512,128]{0,1:T(8,128)(2,1)} %copy.187), channel_id=1, source_target_pairs={{4,0},{8,4},{12,8},{16,12},{20,16},{24,20},{28,24},{0,28},{5,1},{9... | collective-permute-start | bytes 393224 | tf_op jit(solution)/shard_map/while/body/eval_jaxpr/ppermute | solution.py:38
  258.1 22.6 %collective-permute-start.1 = (bf16[512,128]{1,0:T(8,128)(2,1)}, bf16[512,128]{1,0:T(8,128)(2,1)}, u32[]{:S(2)}, u32[]{:S(2)}) collective-permute-start(bf16[512,128]{1,0:T(8,128)(2,1)} %copy.188), channel_id=1, source_target_pairs={{4,0},{8,4},{12,8},{16,12},{20,16},{24,20},{28,24},{0,28},{5,1},{9... | collective-permute-start | bytes 393224 | tf_op jit(solution)/shard_map/while/body/eval_jaxpr/ppermute | solution.py:38
  263.3 17.5 %collective-permute-start.3 = (f32[512,128]{1,0:T(8,128)}, f32[512,128]{1,0:T(8,128)S(1)}, u32[]{:S(2)}, u32[]{:S(2)}) collective-permute-start(f32[512,128]{1,0:T(8,128)} %add.404), channel_id=1, source_target_pairs={{4,0},{8,4},{12,8},{16,12},{20,16},{24,20},{28,24},{0,28},{5,1},{9... | collective-permute-start | bytes 786440 | tf_op jit(solution)/shard_map/while/body/eval_jaxpr/ppermute | solution.py:38
  277.3 5.3 %collective-permute-start.2 = (f32[512,128]{1,0:T(8,128)}, f32[512,128]{1,0:T(8,128)}, u32[]{:S(2)}, u32[]{:S(2)}) collective-permute-start(f32[512,128]{1,0:T(8,128)} %add.403), channel_id=1, source_target_pairs={{4,0},{8,4},{12,8},{16,12},{20,16},{24,20},{28,24},{0,28},{5,1},{9... | collective-permute-start | bytes 786440 | tf_op jit(solution)/shard_map/while/body/eval_jaxpr/ppermute | solution.py:38
  283.2 26.1 %collective-permute-start = (bf16[512,128]{0,1:T(8,128)(2,1)}, bf16[512,128]{0,1:T(8,128)(2,1)S(1)}, u32[]{:S(2)}, u32[]{:S(2)}) collective-permute-start(bf16[512,128]{0,1:T(8,128)(2,1)} %copy.187), channel_id=1, source_target_pairs={{4,0},{8,4},{12,8},{16,12},{20,16},{24,20},{28,24},{0,28},{5,1},{9... | collective-permute-start | bytes 393224 | tf_op jit(solution)/shard_map/while/body/eval_jaxpr/ppermute | solution.py:38
  286.7 22.6 %collective-permute-start.1 = (bf16[512,128]{1,0:T(8,128)(2,1)}, bf16[512,128]{1,0:T(8,128)(2,1)}, u32[]{:S(2)}, u32[]{:S(2)}) collective-permute-start(bf16[512,128]{1,0:T(8,128)(2,1)} %copy.188), channel_id=1, source_target_pairs={{4,0},{8,4},{12,8},{16,12},{20,16},{24,20},{28,24},{0,28},{5,1},{9... | collective-permute-start | bytes 393224 | tf_op jit(solution)/shard_map/while/body/eval_jaxpr/ppermute | solution.py:38
  291.9 17.5 %collective-permute-start.3 = (f32[512,128]{1,0:T(8,128)}, f32[512,128]{1,0:T(8,128)S(1)}, u32[]{:S(2)}, u32[]{:S(2)}) collective-permute-start(f32[512,128]{1,0:T(8,128)} %add.404), channel_id=1, source_target_pairs={{4,0},{8,4},{12,8},{16,12},{20,16},{24,20},{28,24},{0,28},{5,1},{9... | collective-permute-start | bytes 786440 | tf_op jit(solution)/shard_map/while/body/eval_jaxpr/ppermute | solution.py:38
  305.9 5.3 %collective-permute-start.2 = (f32[512,128]{1,0:T(8,128)}, f32[512,128]{1,0:T(8,128)}, u32[]{:S(2)}, u32[]{:S(2)}) collective-permute-start(f32[512,128]{1,0:T(8,128)} %add.403), channel_id=1, source_target_pairs={{4,0},{8,4},{12,8},{16,12},{20,16},{24,20},{28,24},{0,28},{5,1},{9... | collective-permute-start | bytes 786440 | tf_op jit(solution)/shard_map/while/body/eval_jaxpr/ppermute | solution.py:38
  329.0 12.3 %collective-permute-start.13 = (f32[512,128]{1,0:T(8,128)S(1)}, f32[512,128]{1,0:T(8,128)S(1)}, u32[]{:S(2)}, u32[]{:S(2)}) collective-permute-start(f32[512,128]{1,0:T(8,128)S(1)} %add.338), channel_id=1, source_target_pairs={{4,0},{8,4},{12,8},{16,12},{20,16},{24,20},{28,24},{0,28},{5,1},{9... | collective-permute-start | bytes 786440 | tf_op jit(solution)/shard_map/ppermute | solution.py:38
  332.2 4.3 %collective-permute-start.14 = (bf16[512,128]{1,0:T(8,128)(2,1)S(1)}, bf16[512,128]{1,0:T(8,128)(2,1)}, u32[]{:S(2)}, u32[]{:S(2)}) collective-permute-start(bf16[512,128]{1,0:T(8,128)(2,1)S(1)} %add.339), channel_id=1, source_target_pairs={{4,0},{8,4},{12,8},{16,12},{20,16},{24,20},{28,24},{0,28},{5,1},{9... | collective-permute-start | bytes 393224 | tf_op jit(solution)/shard_map/ppermute | solution.py:38
  336.5 11.0 %all-to-all-start.7 = ((bf16[4,128,128]{2,1,0:T(8,128)(2,1)}), bf16[4,128,128]{2,1,0:T(8,128)(2,1)S(1)}, u32[]{:S(2)}, u32[]{:S(2)}) async-start(bf16[4,128,128]{2,1,0:T(8,128)(2,1)} %bitcast.112), calls=%async_computation.7 | async-start | bytes 262144 | tf_op jit(solution)/shard_map/all_to_all | solution.py:196
  347.5 9.2 %all-to-all-start.6 = ((bf16[4,128,128]{2,1,0:T(8,128)(2,1)}), bf16[4,128,128]{2,1,0:T(8,128)(2,1)S(1)}, u32[]{:S(2)}, u32[]{:S(2)}) async-start(bf16[4,128,128]{2,1,0:T(8,128)(2,1)} %bitcast.109), calls=%async_computation.6 | async-start | bytes 262144 | tf_op jit(solution)/shard_map/all_to_all | solution.py:195
  356.7 27.2 %all-to-all-start.5 = ((bf16[4,128,1024]{2,1,0:T(8,128)(2,1)}), bf16[4,128,1024]{2,1,0:T(8,128)(2,1)S(1)}, u32[]{:S(2)}, u32[]{:S(2)}) async-start(bf16[4,128,1024]{2,1,0:T(8,128)(2,1)} %bitcast.106), calls=%async_computation.5 | async-start | bytes 2097152 | tf_op jit(solution)/shard_map/all_to_all | solution.py:194
  (24 other events, 342.0 us)
